TPU v7x, 512 devices: a whole 4x4x16 slice. The times are simulated.
512 devices in a mesh: dp: 32 (over z, core), cent: 16 (over y, x).
Axes of the slice: x: 4, y: 4, z: 16, core: 2. Of those that a mesh axis runs over, the one named last changes fastest.
Arguments:
- points: bfloat16 [131072, 1024], P(('dp', 'cent')), may hold values from -22 to 22, as said below
- block_list: int32 [4096, 3], P(('dp', 'cent')), may hold values from 0 to 15, all different within a row; in each aligned block of 8 rows (0 to 7, 8 to 15, ...) at most 2 rows name the same one
- list_count: int32 [4096], P(('dp', 'cent')), may hold values from 1 to 3
- centroids: bfloat16 [16, 1024, 1024], P('cent', 'dp'), may hold values from -14 to 14, as said below
Outputs:
- new_centroids: float32 [16, 1024, 1024], P('cent', 'dp')
Inputs may be any that keep to these rules, and one draw needn't show every extreme that they name: `block_list`: within the rows of one device (aligned blocks of 8 rows) no block id appears more than 2 times, and the ids of one row differ. Only the first list_count[t] entries of row t of block_list are valid. `points`: Real-valued embeddings. Real-valued centroids.
All inputs are finite; a program needn't handle non-finite values.
Results may differ from a plain program's by a relative error of at most 0.0019.
Values may be sent and summed in bfloat16 or wider, within the bound.
No kernel may reach another device: no remote copies, remote signals or barrier semaphores. Data moves between devices by JAX's collectives and lax.ppermute only.
A program may use at most 64 MiB of HBM per device.

v0:
```python
import math
import jax
import jax.numpy as jnp
from jax import lax
from jax.sharding import PartitionSpec as P

score_scale = 2.0
prior_weight = 1.0


def combine_norms(peaks, totals, usable):
    keep = usable[..., None]
    highest = jnp.max(jnp.where(keep, peaks, -1e30), axis=-2)
    summed = jnp.sum(jnp.where(keep, totals * jnp.exp(peaks - highest[..., None, :]), 0.0), axis=-2)
    return highest + jnp.log(summed)


def per_device(points, block_list, list_count, centroids):
    owners = lax.axis_size("cent")
    tiles_here, listed = block_list.shape
    width = points.shape[1]
    tile_rows = points.shape[0] // tiles_here
    capacity = (tiles_here * listed + owners - 1) // owners
    slot_rows = capacity * tile_rows
    scale = score_scale / math.sqrt(width)
    usable = jnp.arange(listed, dtype=jnp.int32)[None, :] < list_count[:, None]
    naming = jnp.logical_and(
        block_list[:, :, None] == jnp.arange(owners, dtype=jnp.int32)[None, None, :],
        usable[:, :, None],
    )
    listing = jnp.any(naming, axis=1).astype(jnp.int32)
    earlier = jnp.cumsum(listing, axis=0) - listing
    placing = jnp.logical_and(
        listing.T[:, None, :] == 1,
        earlier.T[:, None, :] == jnp.arange(capacity, dtype=jnp.int32)[None, :, None],
    )
    placing = placing.astype(jnp.float32).reshape(owners * capacity, tiles_here)
    slot_rank = jnp.take_along_axis(earlier, block_list, axis=1)
    route_code = jnp.where(usable, block_list * capacity + slot_rank, -1)
    outgoing = jnp.dot(
        placing.astype(jnp.bfloat16),
        points.reshape(tiles_here, tile_rows * width),
        preferred_element_type=jnp.float32,
    )
    outgoing = outgoing.astype(jnp.bfloat16).reshape(owners, slot_rows, width)
    slot_routes = (
        jnp.dot(placing, (route_code + 1).astype(jnp.float32), precision=lax.Precision.HIGHEST)
        - 1.0
    )
    slot_routes = slot_routes.astype(jnp.bfloat16).reshape(owners, capacity, listed)
    arrived, arrived_routes = (
        lax.all_to_all(outgoing, "cent", split_axis=0, concat_axis=0, tiled=True),
        lax.all_to_all(slot_routes, "cent", split_axis=0, concat_axis=0, tiled=True),
    )
    incoming = arrived.reshape(owners * slot_rows, width)
    occupied = arrived_routes[:, :, 0] >= 0
    occupied_rows = jnp.broadcast_to(occupied[:, :, None], (owners, capacity, tile_rows)).reshape(
        -1
    )
    logits = (
        lax.dot_general(
            incoming,
            lax.all_gather(centroids, "dp", axis=1, tiled=True)[0],
            (((1,), (1,)), ((), ())),
            preferred_element_type=jnp.float32,
        )
        * scale
    )
    peaks = jnp.max(logits, axis=1)
    totals = jnp.sum(jnp.exp(logits - peaks[:, None]), axis=1)
    back_peaks, back_totals = (
        lax.all_to_all(
            peaks.reshape(owners, slot_rows), "cent", split_axis=0, concat_axis=0, tiled=True
        ),
        lax.all_to_all(
            totals.reshape(owners, slot_rows), "cent", split_axis=0, concat_axis=0, tiled=True
        ),
    )
    lookup = jnp.where(usable, route_code, 0)
    tile_norms = combine_norms(
        back_peaks.reshape(owners * capacity, tile_rows)[lookup],
        back_totals.reshape(owners * capacity, tile_rows)[lookup],
        usable,
    )
    slot_norms = jnp.dot(placing, tile_norms, precision=lax.Precision.HIGHEST)
    row_norms = lax.all_to_all(
        slot_norms.reshape(owners, slot_rows), "cent", split_axis=0, concat_axis=0, tiled=True
    ).reshape(-1)
    shares = jnp.where(occupied_rows[:, None], jnp.exp(logits - row_norms[:, None]), 0.0).astype(
        jnp.bfloat16
    )
    own_rows = centroids[0].astype(jnp.float32)
    own_count = own_rows.shape[0]
    block_mass = jnp.sum(shares, axis=0, dtype=jnp.float32)
    full_mass = lax.psum(block_mass, "dp")
    new_mass = lax.dynamic_slice_in_dim(full_mass, lax.axis_index("dp") * own_count, own_count, 0)
    block_sums = lax.dot_general(
        shares, incoming, (((0,), (0,)), ((), ())), preferred_element_type=jnp.float32
    )
    new_sums = lax.psum_scatter(block_sums, "dp", scatter_dimension=0, tiled=True)
    fresh = (new_sums + prior_weight * own_rows) / (new_mass[:, None] + prior_weight)
    return fresh[None]


def solution(mesh):
    in_specs = (
        P(("dp", "cent"), None),
        P(("dp", "cent"), None),
        P(("dp", "cent")),
        P("cent", "dp", None),
    )
    out_specs = P("cent", "dp", None)
    return jax.shard_map(
        per_device, mesh=mesh, in_specs=in_specs, out_specs=out_specs, check_vma=False
    )
```

profile of v0, /device:TPU:2, one launch (start us, length us, event | category | flops | bytes accessed | tf_op | source)
XLA Modules:
  0.0 253.5 jit_solution(3150392634497232480)
XLA Ops:
  7.3 0.7 iota_compare_fusion.1
  8.1 0.8 copy.56
  8.8 0.8 fusion.8
  10.2 0.7 gather_fusion.2
  11.4 0.7 copy.66
  12.1 9.2 %all-to-all-start = ((bf16[16,2,3]{2,1,0:T(2,128)(2,1)}), bf16[16,2,3]{2,1,0:T(2,128)(2,1)S(1)}, u32[]{:S(2)}, u32[]{:S(2)}) async-start(bf16[16,2,3]{2,1,0:T(2,128)(2,1)} %bitcast.4), calls=%async_computation | async-start | bytes 16384 | tf_op jit(solution)/shard_map/all_to_all | solution.py:53
  22.2 2.4 reshape.118
  24.6 2.8 %all-to-all-done = bf16[16,2,3]{2,1,0:T(2,128)(2,1)S(1)} async-done(((bf16[16,2,3]{2,1,0:T(2,128)(2,1)}), bf16[16,2,3]{2,1,0:T(2,128)(2,1)S(1)}, u32[]{:S(2)}, u32[]{:S(2)}) %all-to-all-start) | async-done | bytes 224 | tf_op jit(solution)/shard_map/all_to_all | solution.py:53
  27.5 5.0 %all-to-all-start.1 = ((bf16[16,64,1024]{2,1,0:T(8,128)(2,1)}), bf16[16,64,1024]{2,1,0:T(8,128)(2,1)S(1)}, u32[]{:S(2)}, u32[]{:S(2)}) async-start(bf16[16,64,1024]{2,1,0:T(8,128)(2,1)} %reshape.118), calls=%async_computation.1 | async-start | bytes 4194304 | tf_op jit(solution)/shard_map/all_to_all | solution.py:52
  32.7 24.7 %all-to-all-done.1 = bf16[16,64,1024]{2,1,0:T(8,128)(2,1)S(1)} async-done(((bf16[16,64,1024]{2,1,0:T(8,128)(2,1)}), bf16[16,64,1024]{2,1,0:T(8,128)(2,1)S(1)}, u32[]{:S(2)}, u32[]{:S(2)}) %all-to-all-start.1) | async-done | bytes 2097184 | tf_op jit(solution)/shard_map/all_to_all | solution.py:52
  57.4 28.3 %all-gather.2.cloned.1.call-done = bf16[1,1024,1024]{2,1,0:T(8,128)(2,1)} async-done(((bf16[1,32,1024]{2,1,0:T(8,128)(2,1)}), bf16[1,1024,1024]{2,1,0:T(8,128)(2,1)}) %all-gather.2.cloned.1.call-update) | async-done | bytes 2097168 | tf_op jit(solution)/shard_map/all_gather | solution.py:63
  85.7 5.9 %multiply_reduce_fusion = (f32[1024]{0:T(1024)S(1)}, f32[1024,1024]{0,1:T(8,128)}) fusion(bf16[1024,1024]{1,0:T(8,128)(2,1)S(1)} %bitcast.32, bf16[1,1024,1024]{2,1,0:T(8,128)(2,1)} %all-gather.2.cloned.1.call-done), kind=kOutput, calls=%fused_computation.7 | convolution fusion | flops 2149579776 | bytes 8392704 | tf_op jit(solution)/shard_map/dot_general | solution.py:61
  92.3 7.3 %all-to-all-start.2 = ((f32[16,1,64]{2,1,0:T(1,128)}), f32[16,1,64]{2,1,0:T(1,128)S(1)}, u32[]{:S(2)}, u32[]{:S(2)}) async-start(f32[16,1,64]{2,1,0:T(1,128)} %all_to_all.26), calls=%async_computation.2 | async-start | bytes 16384 | tf_op jit(solution)/shard_map/all_to_all | solution.py:72
  99.6 2.9 %exponential_reduce_fusion = f32[1024]{0:T(1024)S(1)} fusion(f32[1024,1024]{0,1:T(8,128)} %get-tuple-element.8, f32[1024]{0:T(1024)S(1)} %get-tuple-element.7), kind=kLoop, calls=%fused_computation.6 | loop fusion | flops 3144704 | bytes 4202496 | tf_op jit(solution)/shard_map/reduce_sum | solution.py:70
  103.2 2.5 all-to-all-done.2
  105.7 4.7 %all-to-all-start.3 = ((f32[16,1,64]{2,1,0:T(1,128)}), f32[16,1,64]{2,1,0:T(1,128)S(1)}, u32[]{:S(2)}, u32[]{:S(2)}) async-start(f32[16,1,64]{2,1,0:T(1,128)} %all_to_all.28), calls=%async_computation.3 | async-start | bytes 16384 | tf_op jit(solution)/shard_map/all_to_all | solution.py:75
  112.4 4.1 %all-to-all-done.3 = f32[16,1,64]{2,1,0:T(1,128)S(1)} async-done(((f32[16,1,64]{2,1,0:T(1,128)}), f32[16,1,64]{2,1,0:T(1,128)S(1)}, u32[]{:S(2)}, u32[]{:S(2)}) %all-to-all-start.3) | async-done | bytes 4128 | tf_op jit(solution)/shard_map/all_to_all | solution.py:75
  118.7 4.9 %all-to-all-start.4 = ((f32[16,1,64]{2,1,0:T(1,128)}), f32[16,1,64]{2,1,0:T(1,128)S(1)}, u32[]{:S(2)}, u32[]{:S(2)}) async-start(f32[16,1,64]{2,1,0:T(1,128)} %bitcast.9), calls=%async_computation.4 | async-start | bytes 16384 | tf_op jit(solution)/shard_map/all_to_all | solution.py:86
  123.9 5.8 %all-to-all-done.4 = f32[16,1,64]{2,1,0:T(1,128)S(1)} async-done(((f32[16,1,64]{2,1,0:T(1,128)}), f32[16,1,64]{2,1,0:T(1,128)S(1)}, u32[]{:S(2)}, u32[]{:S(2)}) %all-to-all-start.4) | async-done | bytes 4128 | tf_op jit(solution)/shard_map/all_to_all | solution.py:86
  130.5 6.5 %fusion.5 = f32[1024,1024]{1,0:T(8,128)} fusion(bf16[1024,1024]{1,0:T(8,128)(2,1)S(1)} %bitcast.33, f32[1024,1024]{0,1:T(8,128)} %get-tuple-element.8, f32[1024]{0:T(1024)S(1)} %sub.44, pred[1024]{0:T(1024)(128)(4,1)S(1)} %broadcast_in_dim.67), kind=kOutput, calls=%fused_computation.15 | convolution fusion | flops 2151677952 | bytes 10490880 | tf_op jit(solution)/shard_map/dot_general | solution.py:97
  137.0 3.1 %convert_reduce_fusion = f32[1024]{0:T(1024)S(1)} fusion(f32[1024]{0:T(1024)S(1)} %sub.44, f32[1024,1024]{0,1:T(8,128)} %get-tuple-element.8, pred[1024]{0:T(1024)(128)(4,1)S(1)} %broadcast_in_dim.67), kind=kLoop, calls=%fused_computation.4 | loop fusion | flops 6290432 | bytes 4203520 | tf_op jit(solution)/shard_map/reduce_sum | solution.py:94
  140.1 45.8 %psum.7 = f32[1024]{0:T(1024)S(1)} all-reduce(f32[1024]{0:T(1024)S(1)} %convert_reduce_fusion), channel_id=1, replica_groups=mesh['dp'=32,'cent'=16] {'dp'}, use_global_device_ids=true, to_apply=%region_8.9 | all-reduce | flops 1024 | bytes 8192 | tf_op jit(solution)/shard_map/psum | solution.py:95
  186.0 59.1 %reduce-scatter.2.cloned.1.call-done = f32[32,1024]{1,0:T(8,128)} async-done(((f32[1024,1024]{1,0:T(8,128)}), f32[32,1024]{1,0:T(8,128)}) %reduce-scatter.2.cloned.1.call-update) | async-done | bytes 131088 | tf_op jit(solution)/shard_map/reduce_scatter | solution.py:100
  245.0 1.6 fusion.4
  (58 shorter events, 9.6 us)
Async XLA Ops:
  6.5 4.6 %copy-start.2 = (s32[8]{0:T(128)S(1)}, s32[8]{0:T(128)}, u32[]{:S(2)}) copy-start(s32[8]{0:T(128)} %param.6) | copy-start | bytes 100
  6.5 14.7 %copy-start = (bf16[256,1024]{1,0:T(8,128)(2,1)S(1)}, bf16[256,1024]{1,0:T(8,128)(2,1)}, u32[]{:S(2)}) copy-start(bf16[256,1024]{1,0:T(8,128)(2,1)} %param.4) | copy-start | bytes 1572868
  6.5 79.2 %all-gather.2.cloned.1.call-start = ((), (), s32[]{:S(2)}) async-start(), calls=%async_computation.6 | async-start | bytes 2162688 | tf_op jit(solution)/shard_map/all_gather | solution.py:63
  12.1 15.3 %all-to-all-start = ((bf16[16,2,3]{2,1,0:T(2,128)(2,1)}), bf16[16,2,3]{2,1,0:T(2,128)(2,1)S(1)}, u32[]{:S(2)}, u32[]{:S(2)}) async-start(bf16[16,2,3]{2,1,0:T(2,128)(2,1)} %bitcast.4), calls=%async_computation | async-start | bytes 16384 | tf_op jit(solution)/shard_map/all_to_all | solution.py:53
  27.5 29.9 %all-to-all-start.1 = ((bf16[16,64,1024]{2,1,0:T(8,128)(2,1)}), bf16[16,64,1024]{2,1,0:T(8,128)(2,1)S(1)}, u32[]{:S(2)}, u32[]{:S(2)}) async-start(bf16[16,64,1024]{2,1,0:T(8,128)(2,1)} %reshape.118), calls=%async_computation.1 | async-start | bytes 4194304 | tf_op jit(solution)/shard_map/all_to_all | solution.py:52
  92.3 13.4 %all-to-all-start.2 = ((f32[16,1,64]{2,1,0:T(1,128)}), f32[16,1,64]{2,1,0:T(1,128)S(1)}, u32[]{:S(2)}, u32[]{:S(2)}) async-start(f32[16,1,64]{2,1,0:T(1,128)} %all_to_all.26), calls=%async_computation.2 | async-start | bytes 16384 | tf_op jit(solution)/shard_map/all_to_all | solution.py:72
  105.7 10.8 %all-to-all-start.3 = ((f32[16,1,64]{2,1,0:T(1,128)}), f32[16,1,64]{2,1,0:T(1,128)S(1)}, u32[]{:S(2)}, u32[]{:S(2)}) async-start(f32[16,1,64]{2,1,0:T(1,128)} %all_to_all.28), calls=%async_computation.3 | async-start | bytes 16384 | tf_op jit(solution)/shard_map/all_to_all | solution.py:75
  118.7 11.0 %all-to-all-start.4 = ((f32[16,1,64]{2,1,0:T(1,128)}), f32[16,1,64]{2,1,0:T(1,128)S(1)}, u32[]{:S(2)}, u32[]{:S(2)}) async-start(f32[16,1,64]{2,1,0:T(1,128)} %bitcast.9), calls=%async_computation.4 | async-start | bytes 16384 | tf_op jit(solution)/shard_map/all_to_all | solution.py:86
  123.6 121.5 %reduce-scatter.2.cloned.1.call-start = ((), (), s32[]{:S(2)}) async-start(), calls=%async_computation.7 | async-start | bytes 4325376 | tf_op jit(solution)/shard_map/reduce_scatter | solution.py:100
  137.0 108.1 %copy-start.1 = (bf16[1,32,1024]{2,1,0:T(8,128)(2,1)S(1)}, bf16[1,32,1024]{2,1,0:T(8,128)(2,1)}, u32[]{:S(2)}) copy-start(bf16[1,32,1024]{2,1,0:T(8,128)(2,1)} %param.7) | copy-start | bytes 196612
Sparse Core Ops, SparseCore 0:
  9.5 76.2 all-gather.1
  137.1 107.8 reduce-scatter.1
where the time goes:
time: 254 us
  waiting for transfers between devices  128 us (50%)
  blocking collectives  45.8 us (18%)
  starting transfers between devices  31.1 us (12%)
  between operations  13.5 us (5%)
  matrix products  13.4 us (5%)
  other arithmetic  11.5 us (5%)
  local copies, waits for them, and re-layouts  9.97 us (4%)
    reduce_scatter x1, waiting for transfers between devices, per_device(): lax.psum_scatter(block_sums, 'dp', scatter_dimension=0, tiled=True)  59.1 us
    psum x1, blocking collectives, per_device(): full_mass = lax.psum(block_mass, 'dp')  45.8 us
    all_gather x1, waiting for transfers between devices, per_device(): lax.all_gather(centroids, 'dp', axis=1, tiled=True)[0]  28.3 us
    all_to_all x1, waiting for transfers between devices, per_device(): lax.all_to_all(outgoing, 'cent', split_axis=0, concat_axis=0, tiled=True)  24.7 us
    all_to_all x1, starting transfers between devices, per_device(): lax.all_to_all(slot_routes, 'cent', split_axis=0, concat_axis=0, tiled=True)  9.17 us
    all_to_all x1, starting transfers between devices, per_device(): lax.all_to_all(peaks.reshape(owners, slot_rows), 'cent', split_axis=0, co...  7.32 us
    dot_general x1, matrix products, per_device(): lax.dot_general(shares, incoming, (((0,), (0,)), ((), ())), preferred_ele...  6.49 us
    dot_general x1, matrix products, per_device(): lax.dot_general(incoming, lax.all_gather(centroids, 'dp', axis=1, tiled=T...  5.89 us
  transfers between devices with their start and end apart: 7, of which 7 were waited for; matrix products, arithmetic and copies ran while one was open for 7% of the time, Pallas kernels for 0%

commit v1 on v0

--- a/solution.py
+++ b/solution.py
@@ -57,10 +57,14 @@
     occupied_rows = jnp.broadcast_to(occupied[:, :, None], (owners, capacity, tile_rows)).reshape(
         -1
     )
+    _open_results = lambda mine: jnp.concatenate(
+        lax.all_to_all(jnp.stack([mine for _ in range(lax.axis_size("dp"))], axis=0), "dp", 0, 0),
+        axis=1,
+    )
     logits = (
         lax.dot_general(
             incoming,
-            lax.all_gather(centroids, "dp", axis=1, tiled=True)[0],
+            _open_results(centroids)[0],
             (((1,), (1,)), ((), ())),
             preferred_element_type=jnp.float32,
         )

time: 254 us -> 336 us (1.32)
  the two profiles are of different devices: /device:TPU:2 before, /device:TPU:4 now
where the time goes in v1:
time: 336 us; the launch traced here: 335 us
  waiting for transfers between devices  167 us (50%)
  blocking collectives  74.7 us (22%)
  starting transfers between devices  42.6 us (13%)
  between operations  13.6 us (4%)
  matrix products  13.4 us (4%)
  local copies, waits for them, and re-layouts  11.6 us (3%)
  other arithmetic  11.6 us (3%)
    all_to_all x1, waiting for transfers between devices, per_device(): lax.all_to_all(jnp.stack([mine for _ in range(lax.axis_size('dp'))], axis...  98.9 us
    reduce_scatter x1, waiting for transfers between devices, per_device(): lax.psum_scatter(block_sums, 'dp', scatter_dimension=0, tiled=True)  56.5 us
    psum x1, blocking collectives, per_device(): full_mass = lax.psum(block_mass, 'dp')  45.9 us
    all_to_all x1, blocking collectives, per_device(): lax.all_to_all(outgoing, 'cent', split_axis=0, concat_axis=0, tiled=True)  28.8 us
    all_to_all x1, starting transfers between devices, per_device(): lax.all_to_all(jnp.stack([mine for _ in range(lax.axis_size('dp'))], axis...  16.1 us
    all_to_all x1, starting transfers between devices, per_device(): lax.all_to_all(slot_routes, 'cent', split_axis=0, concat_axis=0, tiled=True)  9.15 us
  transfers between devices with their start and end apart: 6, of which 6 were waited for; matrix products, arithmetic and copies ran while one was open for 4% of the time, Pallas kernels for 0%

profile of v1, /device:TPU:4, one launch (start us, length us, event | category | flops | bytes accessed | tf_op | source)
XLA Modules:
  0.0 334.9 jit_solution(10831791050277216166)
XLA Ops:
  6.5 0.8 iota_compare_fusion.1
  7.4 0.8 copy.56
  8.2 0.8 fusion.4
  9.6 0.7 gather_fusion.2
  11.5 9.1 %all-to-all-start = ((bf16[16,2,3]{2,1,0:T(2,128)(2,1)}), bf16[16,2,3]{2,1,0:T(2,128)(2,1)S(1)}, u32[]{:S(2)}, u32[]{:S(2)}) async-start(bf16[16,2,3]{2,1,0:T(2,128)(2,1)} %bitcast.4), calls=%async_computation | async-start | bytes 16384 | tf_op jit(solution)/shard_map/all_to_all | solution.py:53
  21.6 2.4 reshape.119
  24.0 1.9 all-to-all-done
  25.9 28.8 %all_to_all.42 = bf16[16,64,1024]{2,1,0:T(8,128)(2,1)S(1)} all-to-all(bf16[16,64,1024]{2,1,0:T(8,128)(2,1)} %reshape.119), channel_id=1, replica_groups=mesh['dp'=32,'cent'=16] {'cent'}, dimensions={0} | all-to-all | bytes 4194304 | tf_op jit(solution)/shard_map/all_to_all | solution.py:52
  54.7 1.6 stack.2
  56.3 16.1 %all-to-all-start.2 = ((bf16[32,1,32,1024]{3,2,1,0:T(8,128)(2,1)}), bf16[32,1,32,1024]{3,2,1,0:T(8,128)(2,1)}, u32[]{:S(2)}, u32[]{:S(2)}) async-start(bf16[32,1,32,1024]{3,2,1,0:T(8,128)(2,1)} %stack.2), calls=%async_computation.2 | async-start | bytes 4194304 | tf_op jit(solution)/shard_map/all_to_all | solution.py:61
  72.7 98.9 %all-to-all-done.2 = bf16[32,1,32,1024]{3,2,1,0:T(8,128)(2,1)} async-done(((bf16[32,1,32,1024]{3,2,1,0:T(8,128)(2,1)}), bf16[32,1,32,1024]{3,2,1,0:T(8,128)(2,1)}, u32[]{:S(2)}, u32[]{:S(2)}) %all-to-all-start.2) | async-done | bytes 2097184 | tf_op jit(solution)/shard_map/all_to_all | solution.py:61
  171.7 5.9 %multiply_reduce_fusion = (f32[1024]{0:T(1024)S(1)}, f32[1024,1024]{0,1:T(8,128)}) fusion(bf16[1024,1024]{1,0:T(8,128)(2,1)S(1)} %bitcast.28, bf16[1024,1024]{1,0:T(8,128)(2,1)} %bitcast.9), kind=kOutput, calls=%fused_computation.7 | convolution fusion | flops 2149579776 | bytes 8392704 | tf_op jit(solution)/shard_map/dot_general | solution.py:65
  178.2 6.1 %all-to-all-start.3 = ((f32[16,1,64]{2,1,0:T(1,128)}), f32[16,1,64]{2,1,0:T(1,128)S(1)}, u32[]{:S(2)}, u32[]{:S(2)}) async-start(f32[16,1,64]{2,1,0:T(1,128)} %all_to_all.30), calls=%async_computation.3 | async-start | bytes 16384 | tf_op jit(solution)/shard_map/all_to_all | solution.py:76
  184.4 2.9 exponential_reduce_fusion
  188.0 1.7 all-to-all-done.3
  189.7 5.6 %all-to-all-start.4 = ((f32[16,1,64]{2,1,0:T(1,128)}), f32[16,1,64]{2,1,0:T(1,128)S(1)}, u32[]{:S(2)}, u32[]{:S(2)}) async-start(f32[16,1,64]{2,1,0:T(1,128)} %all_to_all.32), calls=%async_computation.4 | async-start | bytes 16384 | tf_op jit(solution)/shard_map/all_to_all | solution.py:79
  197.2 3.4 %all-to-all-done.4 = f32[16,1,64]{2,1,0:T(1,128)S(1)} async-done(((f32[16,1,64]{2,1,0:T(1,128)}), f32[16,1,64]{2,1,0:T(1,128)S(1)}, u32[]{:S(2)}, u32[]{:S(2)}) %all-to-all-start.4) | async-done | bytes 4128 | tf_op jit(solution)/shard_map/all_to_all | solution.py:79
  202.8 5.6 %all-to-all-start.5 = ((f32[16,1,64]{2,1,0:T(1,128)}), f32[16,1,64]{2,1,0:T(1,128)S(1)}, u32[]{:S(2)}, u32[]{:S(2)}) async-start(f32[16,1,64]{2,1,0:T(1,128)} %bitcast.10), calls=%async_computation.5 | async-start | bytes 16384 | tf_op jit(solution)/shard_map/all_to_all | solution.py:90
  208.7 5.0 %all-to-all-done.5 = f32[16,1,64]{2,1,0:T(1,128)S(1)} async-done(((f32[16,1,64]{2,1,0:T(1,128)}), f32[16,1,64]{2,1,0:T(1,128)S(1)}, u32[]{:S(2)}, u32[]{:S(2)}) %all-to-all-start.5) | async-done | bytes 4128 | tf_op jit(solution)/shard_map/all_to_all | solution.py:90
  214.4 6.5 %fusion.1 = f32[1024,1024]{1,0:T(8,128)} fusion(bf16[1024,1024]{1,0:T(8,128)(2,1)S(1)} %bitcast.29, f32[1024,1024]{0,1:T(8,128)} %get-tuple-element.8, f32[1024]{0:T(1024)S(1)} %sub.44, pred[1024]{0:T(1024)(128)(4,1)S(1)} %broadcast_in_dim.67), kind=kOutput, calls=%fused_computation.11 | convolution fusion | flops 2151677952 | bytes 10490880 | tf_op jit(solution)/shard_map/dot_general | solution.py:101
  220.9 3.1 convert_reduce_fusion
  224.0 45.9 %psum.7 = f32[1024]{0:T(1024)S(1)} all-reduce(f32[1024]{0:T(1024)S(1)} %convert_reduce_fusion), channel_id=1, replica_groups=mesh['dp'=32,'cent'=16] {'dp'}, use_global_device_ids=true, to_apply=%region_8.9 | all-reduce | flops 1024 | bytes 8192 | tf_op jit(solution)/shard_map/psum | solution.py:99
  270.0 56.5 %reduce-scatter.2.cloned.1.call-done = f32[32,1024]{1,0:T(8,128)} async-done(((f32[1024,1024]{1,0:T(8,128)}), f32[32,1024]{1,0:T(8,128)}) %reduce-scatter.2.cloned.1.call-update) | async-done | bytes 131088 | tf_op jit(solution)/shard_map/reduce_scatter | solution.py:104
  326.4 1.6 divide_bitcast_fusion
  (57 shorter events, 9.6 us)
Async XLA Ops:
  6.5 4.0 %copy-start.2 = (s32[8]{0:T(128)S(1)}, s32[8]{0:T(128)}, u32[]{:S(2)}) copy-start(s32[8]{0:T(128)} %param.6) | copy-start | bytes 100
  6.5 14.1 %copy-start = (bf16[256,1024]{1,0:T(8,128)(2,1)S(1)}, bf16[256,1024]{1,0:T(8,128)(2,1)}, u32[]{:S(2)}) copy-start(bf16[256,1024]{1,0:T(8,128)(2,1)} %param.4) | copy-start | bytes 1572868
  11.5 14.4 %all-to-all-start = ((bf16[16,2,3]{2,1,0:T(2,128)(2,1)}), bf16[16,2,3]{2,1,0:T(2,128)(2,1)S(1)}, u32[]{:S(2)}, u32[]{:S(2)}) async-start(bf16[16,2,3]{2,1,0:T(2,128)(2,1)} %bitcast.4), calls=%async_computation | async-start | bytes 16384 | tf_op jit(solution)/shard_map/all_to_all | solution.py:53
  21.6 33.1 %copy-start.1 = (bf16[1,32,1024]{2,1,0:T(8,128)(2,1)S(1)}, bf16[1,32,1024]{2,1,0:T(8,128)(2,1)}, u32[]{:S(2)}) copy-start(bf16[1,32,1024]{2,1,0:T(8,128)(2,1)} %param.7) | copy-start | bytes 196612
  56.3 115.4 %all-to-all-start.2 = ((bf16[32,1,32,1024]{3,2,1,0:T(8,128)(2,1)}), bf16[32,1,32,1024]{3,2,1,0:T(8,128)(2,1)}, u32[]{:S(2)}, u32[]{:S(2)}) async-start(bf16[32,1,32,1024]{3,2,1,0:T(8,128)(2,1)} %stack.2), calls=%async_computation.2 | async-start | bytes 4194304 | tf_op jit(solution)/shard_map/all_to_all | solution.py:61
  178.2 11.4 %all-to-all-start.3 = ((f32[16,1,64]{2,1,0:T(1,128)}), f32[16,1,64]{2,1,0:T(1,128)S(1)}, u32[]{:S(2)}, u32[]{:S(2)}) async-start(f32[16,1,64]{2,1,0:T(1,128)} %all_to_all.30), calls=%async_computation.3 | async-start | bytes 16384 | tf_op jit(solution)/shard_map/all_to_all | solution.py:76
  189.7 10.9 %all-to-all-start.4 = ((f32[16,1,64]{2,1,0:T(1,128)}), f32[16,1,64]{2,1,0:T(1,128)S(1)}, u32[]{:S(2)}, u32[]{:S(2)}) async-start(f32[16,1,64]{2,1,0:T(1,128)} %all_to_all.32), calls=%async_computation.4 | async-start | bytes 16384 | tf_op jit(solution)/shard_map/all_to_all | solution.py:79
  202.8 10.9 %all-to-all-start.5 = ((f32[16,1,64]{2,1,0:T(1,128)}), f32[16,1,64]{2,1,0:T(1,128)S(1)}, u32[]{:S(2)}, u32[]{:S(2)}) async-start(f32[16,1,64]{2,1,0:T(1,128)} %bitcast.10), calls=%async_computation.5 | async-start | bytes 16384 | tf_op jit(solution)/shard_map/all_to_all | solution.py:90
  208.4 118.1 %reduce-scatter.2.cloned.1.call-start = ((), (), s32[]{:S(2)}) async-start(), calls=%async_computation.7 | async-start | bytes 4325376 | tf_op jit(solution)/shard_map/reduce_scatter | solution.py:104
Sparse Core Ops, SparseCore 0:
  221.0 105.3 reduce-scatter.1
